TPU v7x, 256 devices: a whole 4x4x8 slice. The times are simulated.
256 devices in a mesh: group: 8 (over y, core), dev: 32 (over x, z).
Axes of the slice: x: 4, y: 4, z: 8, core: 2. Of those that a mesh axis runs over, the one named last changes fastest.
Arguments:
- embeddings: bfloat16 [262144, 768], P(('group', 'dev')), may hold values from -6 to 6
- cluster_ids: int32 [1024], P(('group', 'dev')), may hold values from 0 to 1023, as said below
Outputs:
- nearest: float32 [262144], P(('group', 'dev'))
Inputs may be any that keep to these rules, and one draw needn't show every extreme that they name: `cluster_ids`: each cluster is a run of 1 to 29 consecutive blocks inside one cluster group of 128 blocks (a group's first block starts a cluster, its last block is a cluster of one block), and its id is the index of its first block; some cluster of every group has exactly 29 blocks.
All inputs are finite; a program needn't handle non-finite values.
Results may differ from a plain program's by a relative error of at most 0.0012.
Values may be sent and summed in bfloat16 or wider, within the bound.
No kernel may reach another device: no remote copies, remote signals or barrier semaphores. Data moves between devices by JAX's collectives and lax.ppermute only.
A program may use at most 192 MiB of HBM per device.

v0:
```python
import jax
import jax.numpy as jnp
from jax import lax
from jax.sharding import PartitionSpec as P


def shift(value, axis, steps, cyclic=False):
    count = lax.axis_size(axis)
    if cyclic:
        pairs = [(source, (source + steps) % count) for source in range(count)]
    else:
        pairs = [(source, source + steps) for source in range(max(0, -steps), min(count, count - steps))]
    return lax.ppermute(value, axis, pairs)


def unit_rows(embeddings):
    values_f = embeddings.astype(jnp.float32)
    squares = jnp.sum(values_f * values_f, axis=1, keepdims=True)
    return (values_f * lax.rsqrt(squares + 1e-06)).astype(jnp.bfloat16)


def body(embeddings, cluster_ids):
    rows, dim = embeddings.shape
    blocks = cluster_ids.shape[0]
    width = rows // blocks
    half = blocks // 2
    count = lax.axis_size("dev")
    stride = count // 4
    place = lax.axis_index("dev")
    first_block = (lax.axis_index("group") * count + place) * blocks
    unit = unit_rows(embeddings)

    own_tags = jnp.repeat(cluster_ids, width)
    local = jnp.arange(rows, dtype=jnp.int32)
    scores = jnp.dot(unit, unit.T, preferred_element_type=jnp.float32)
    keep = (own_tags[:, None] == own_tags[None, :]) & (local[:, None] != local[None, :])
    best = jnp.max(jnp.where(keep, scores + 2.0, jnp.zeros_like(scores)), axis=1)

    lag = first_block + jnp.arange(blocks, dtype=jnp.int32) - cluster_ids
    meta = jnp.zeros((16, dim), jnp.bfloat16).at[0, :blocks].set(lag.astype(jnp.bfloat16))
    extra = meta.shape[0]
    packet = jnp.concatenate([unit, meta], axis=0)
    everything = tuple(range(blocks))
    low, high = everything[:half], everything[half:]

    def part(pk, chosen):
        return jnp.concatenate([pk[chosen[0] * width:(chosen[-1] + 1) * width], pk[-extra:]], axis=0)

    def tile(a, a_blocks, b, b_blocks, k, valid):
        nb = len(b_blocks)
        lags = b[nb * width, b_blocks[0]:b_blocks[-1] + 1].astype(jnp.int32)
        block_reach = k * blocks + jnp.array(b_blocks, jnp.int32) - lags
        a_rows = jnp.concatenate([
            jnp.repeat(jnp.array(a_blocks, jnp.int32), width),
            jnp.full((a.shape[0] - len(a_blocks) * width,), -4 * rows, jnp.int32)])
        b_rows = jnp.concatenate([
            jnp.repeat(block_reach, width),
            jnp.full((b.shape[0] - nb * width,), 4 * rows, jnp.int32)])
        matched = (jnp.min(block_reach) <= max(a_blocks)) & valid

        def compute(unused):
            sims = jnp.dot(a, b.T, preferred_element_type=jnp.float32)
            same = b_rows[None, :] <= a_rows[:, None]
            shifted = jnp.where(same, sims + 2.0, jnp.zeros_like(sims))
            return (jnp.max(shifted, axis=1)[: len(a_blocks) * width],
                    jnp.max(shifted, axis=0)[: nb * width])

        def skipped(unused):
            return (jnp.zeros((len(a_blocks) * width,), jnp.float32),
                    jnp.zeros((nb * width,), jnp.float32))

        return lax.cond(matched, compute, skipped, 0)

    far_halves = [shift(unit[:half * width], "dev", stride, cyclic=True),
                  shift(unit[half * width:], "dev", stride, cyclic=True)]
    far = None
    far_ok = [(place >= stride) | (place < m) for m in range(4)]
    ahead = [packet]
    behind = [packet]
    def plan_of():
        return [
            (1, ("own",), everything, ("ahead", 1), everything, 1, True, ("best",), ("ahead", 1)),
            (1, ("behind", 1), everything, ("ahead", 1), everything, 2, place >= 1, ("behind", 1), ("ahead", 1)),
            (2, ("behind", 1), everything, ("ahead", 2), everything, 3, place >= 1, ("behind", 1), ("ahead", 2)),
            (2, ("behind", 2), everything, ("ahead", 2), everything, 4, place >= 2, ("behind", 2), ("ahead", 2)),
            (2, ("far",), everything, ("behind", 1), everything, stride - 1, far_ok[1], ("far",), ("behind", 1)),
            (2, ("far",), everything, ("behind", 2), everything, stride - 2, far_ok[2], ("far",), ("behind", 2)),
            (3, ("behind", 2), everything, ("ahead", 3), low, 5, place >= 2, ("behind", 2), ("ahead", 3)),
            (3, ("far",), everything, ("behind", 3), high, stride - 3, far_ok[3], ("far",), ("behind", 3)),
        ]

    def fetch(where):
        if where[0] == "own":
            return unit
        if where[0] == "far":
            return far
        return (ahead if where[0] == "ahead" else behind)[where[1]]

    sends = {}

    def gather(dest, chosen, value):
        nonlocal best
        if dest == ("best",):
            best = best.at[chosen[0] * width:(chosen[-1] + 1) * width].max(value)
        elif dest in sends:
            sends[dest] = (chosen, jnp.maximum(sends[dest][1], value))
        else:
            sends[dest] = (chosen, value)

    hops = 3
    plan = plan_of()
    for hop in range(1, hops + 1):
        if hop < hops:
            a_next = shift(ahead[-1], "dev", -1)
            b_next = shift(behind[-1], "dev", 1, cyclic=True)
        else:
            a_next = shift(part(ahead[-1], low), "dev", -1)
            b_next = shift(part(behind[-1], high), "dev", 1, cyclic=True)
        ready = [entry for entry in plan if entry[0] == hop - 1]
        pieces = [tile(fetch(e[1]), e[2], fetch(e[3]), e[4], e[5], e[6]) for e in ready]
        if hop == 1:
            a_next, b_next, first, best = lax.optimization_barrier((a_next, b_next, far_halves[0], best))
        elif hop == 2:
            a_next, b_next, second, pieces = lax.optimization_barrier((a_next, b_next, far_halves[1], pieces))
            far = jnp.concatenate([first, second], axis=0)
        else:
            a_next, b_next, pieces = lax.optimization_barrier((a_next, b_next, pieces))
        for e, (row_part, column_part) in zip(ready, pieces):
            gather(e[7], e[2], row_part)
            gather(e[8], e[4], column_part)
        ahead.append(a_next)
        behind.append(b_next)
    ready = [entry for entry in plan if entry[0] == hops]
    for e in ready:
        row_part, column_part = tile(fetch(e[1]), e[2], fetch(e[3]), e[4], e[5], e[6])
        gather(e[7], e[2], row_part)
        gather(e[8], e[4], column_part)

    for dest, (chosen, value) in sends.items():
        if dest[0] == "ahead":
            arrived = shift(value, "dev", dest[1])
        elif dest[0] == "behind":
            arrived = shift(value, "dev", -dest[1], cyclic=True)
        else:
            arrived = shift(value, "dev", -stride, cyclic=True)
        best = best.at[chosen[0] * width:(chosen[-1] + 1) * width].max(arrived)
    return best - 2.0


def solution(mesh):
    return jax.shard_map(
        body,
        mesh=mesh,
        in_specs=(P(("group", "dev"), None), P(("group", "dev"))),
        out_specs=P(("group", "dev")),
        check_vma=False,
    )
```

profile of v0, /device:TPU:4, one launch (start us, length us, event | category | flops | bytes accessed | tf_op | source)
XLA Modules:
  0.0 173.5 jit_solution(14602394888888474619)
XLA Ops:
  0.0 1.9 %fusion.11 = f32[1024]{0:T(1024)S(1)} fusion(bf16[1024,768]{1,0:T(8,128)(2,1)} %param.64), kind=kLoop, calls=%fused_computation.40 | loop fusion | flops 2358272 | bytes 1576960 | tf_op jit(solution)/shard_map/reduce_sum | solution.py:18
  1.9 0.3 fusion.12
  2.3 0.3 copy-done.2
  2.6 0.1 fusion.13
  2.7 7.7 %collective-permute-start = (bf16[1040,768]{1,0:T(8,128)(2,1)S(1)}, bf16[1040,768]{1,0:T(8,128)(2,1)}, u32[]{:S(2)}, u32[]{:S(2)}) collective-permute-start(bf16[1040,768]{1,0:T(8,128)(2,1)S(1)} %fusion.13), channel_id=1, source_target_pairs={{1,0},{2,1},{3,2},{4,3},{5,4},{6,5},{7,6},{8,7},{9,8},{10,9},{11,1... | collective-permute-start | bytes 4792328 | tf_op jit(solution)/shard_map/ppermute | solution.py:13
  10.4 0.1 collective-permute-start.1
  10.5 1.0 fusion.36
  11.5 1.5 collective-permute-start.2
  13.1 2.0 %select_reduce_fusion = f32[1024]{0:T(1024)S(1)} fusion(s32[1024]{0:T(1024)S(1)} %bitcast.120, bf16[1024,768]{1,0:T(8,128)(2,1)S(1)} %fusion.12), kind=kOutput, calls=%fused_computation.33 | convolution fusion | flops 1616903168 | bytes 1581056 | tf_op jit(solution)/shard_map/dot_general | solution.py:35
  15.1 49.6 %collective-permute-done.2 = bf16[512,768]{1,0:T(8,128)(2,1)S(1)} collective-permute-done((bf16[512,768]{1,0:T(8,128)(2,1)S(1)}, bf16[512,768]{1,0:T(8,128)(2,1)S(1)}, u32[]{:S(2)}, u32[]{:S(2)}) %collective-permute-start.2) | collective-permute-done | bytes 786464 | tf_op jit(solution)/shard_map/ppermute | solution.py:13
  64.8 6.0 %collective-permute-start.3 = (bf16[1040,768]{1,0:T(8,128)(2,1)}, bf16[1040,768]{1,0:T(8,128)(2,1)}, u32[]{:S(2)}, u32[]{:S(2)}) collective-permute-start(bf16[1040,768]{1,0:T(8,128)(2,1)} %collective-permute-done), channel_id=1, source_target_pairs={{1,0},{2,1},{3,2},{4,3},{5,4},{6,5},{7,6},{8,7},{9,8},{10,9},{11,1... | collective-permute-start | bytes 4792328 | tf_op jit(solution)/shard_map/ppermute | solution.py:13
  70.8 1.6 collective-permute-start.5
  72.4 1.4 fusion.18
  75.0 4.4 %conditional.9 = (f32[1024]{0:T(1024)S(1)}, f32[1024]{0:T(1024)S(1)}) conditional(s32[]{:T(128)} %convert_element_type.77, () %tuple.129, (s32[4]{0:T(128)S(1)}, s32[4]{0:T(128)S(1)}, bf16[1040,768]{1,0:T(8,128)(2,1)}, bf16[1040,768]{1,0:T(8,128)(2,1)}) %tuple.130), branch_computations={%region_8.9_spmd, %region_9.0_spmd} | conditional | flops 1666743552 | bytes 3269048 | solution.py:72
  75.2 4.3 %fusion.30 = (f32[1040]{0:T(1024)S(1)}, f32[1040]{0:T(1024)S(1)}) fusion(bf16[1040,768]{1,0:T(8,128)(2,1)} %get-tuple-element.283, bf16[1040,768]{1,0:T(8,128)(2,1)} %get-tuple-element.284, s32[1040]{0:T(1024)S(1)} %concatenate.52, s32[1040]{0:T(1024)S(1)} %concatenate.51), kind=kOutput, calls=%fused_computation.80 | convolution fusion | flops 1666743552 | bytes 3211520 | tf_op jit(solution)/shard_map/cond/branch_1_fun/dot_general | solution.py:62
  79.5 3.6 %conditional.8 = (f32[1024]{0:T(1024)S(1)}, f32[1024]{0:T(1024)S(1)}) conditional(s32[]{:T(128)} %convert_element_type.76, () %tuple.127, (s32[4]{0:T(128)S(1)}, s32[4]{0:T(128)S(1)}, bf16[1024,768]{1,0:T(8,128)(2,1)S(1)}, bf16[1040,768]{1,0:T(8,128)(2,1)}) %tuple.128), branch_computations={%region_3.4_spmd, %region_4.7_spmd} | conditional | flops 1641101312 | bytes 3227892 | solution.py:72
  79.6 3.5 %fusion.29 = (f32[1040]{0:T(1024)S(1)}, f32[1024]{0:T(1024)S(1)}) fusion(bf16[1024,768]{1,0:T(8,128)(2,1)S(1)} %get-tuple-element.279, bf16[1040,768]{1,0:T(8,128)(2,1)} %get-tuple-element.280, s32[1024]{0:T(1024)S(1)} %bitcast.117, s32[1040]{0:T(1024)S(1)} %concatenate.50), kind=kOutput, calls=%fused_computation.79 | convolution fusion | flops 1641101312 | bytes 3186816 | tf_op jit(solution)/shard_map/cond/branch_1_fun/dot_general | solution.py:62
  83.1 36.6 %collective-permute-done.5 = bf16[512,768]{1,0:T(8,128)(2,1)S(1)} collective-permute-done((bf16[512,768]{1,0:T(8,128)(2,1)}, bf16[512,768]{1,0:T(8,128)(2,1)S(1)}, u32[]{:S(2)}, u32[]{:S(2)}) %collective-permute-start.5) | collective-permute-done | bytes 786464 | tf_op jit(solution)/shard_map/ppermute | solution.py:13
  119.7 1.2 slice.172
  120.9 0.7 slice.173
  121.7 1.9 %collective-permute-start.7 = (bf16[528,768]{1,0:T(8,128)(2,1)S(1)}, bf16[528,768]{1,0:T(8,128)(2,1)}, u32[]{:S(2)}, u32[]{:S(2)}) collective-permute-start(bf16[528,768]{1,0:T(8,128)(2,1)S(1)} %pad_maximum_fusion), channel_id=1, source_target_pairs={{1,0},{2,1},{3,2},{4,3},{5,4},{6,5},{7,6},{8,7},{9,8},{10,9},{11,1... | collective-permute-start | bytes 2433032 | tf_op jit(solution)/shard_map/ppermute | solution.py:13
  123.6 1.2 concatenate.68
  124.8 2.1 %collective-permute-start.8 = (bf16[528,768]{1,0:T(8,128)(2,1)S(1)}, bf16[528,768]{1,0:T(8,128)(2,1)}, u32[]{:S(2)}, u32[]{:S(2)}) collective-permute-start(bf16[528,768]{1,0:T(8,128)(2,1)S(1)} %concatenate.68), channel_id=1, source_target_pairs={{0,1},{1,2},{2,3},{3,4},{4,5},{5,6},{6,7},{7,8},{8,9},{9,10},{10,1... | collective-permute-start | bytes 2433032 | tf_op jit(solution)/shard_map/ppermute | solution.py:13
  127.5 0.9 constant_dynamic-update-slice_fusion.1
  128.5 1.9 %collective-permute-start.6 = (f32[1024]{0:T(1024)S(1)}, f32[1024]{0:T(1024)S(1)}, u32[]{:S(2)}, u32[]{:S(2)}) collective-permute-start(f32[1024]{0:T(1024)S(1)} %max.71), channel_id=1, source_target_pairs={{0,1},{1,2},{2,3},{3,4},{4,5},{5,6},{6,7},{7,8},{8,9},{9,10},{10,1... | collective-permute-start | bytes 12296 | tf_op jit(solution)/shard_map/ppermute | solution.py:13
  130.4 1.3 fusion.19
  132.4 0.9 constant_dynamic-update-slice_fusion
  133.3 1.4 fusion.25
  136.0 0.2 conditional.13
  136.3 4.4 %conditional.11 = (f32[1024]{0:T(1024)S(1)}, f32[1024]{0:T(1024)S(1)}) conditional(s32[]{:T(128)} %convert_element_type.81, () %tuple.134, (s32[4]{0:T(128)S(1)}, s32[4]{0:T(128)S(1)}, bf16[1040,768]{1,0:T(8,128)(2,1)}, bf16[1040,768]{1,0:T(8,128)(2,1)}) %tuple.135), branch_computations={%region_18.19_spmd, %region_19.22_spmd} | conditional | flops 1666743552 | bytes 3269048 | solution.py:72
  136.4 4.3 %fusion.32 = (f32[1040]{0:T(1024)S(1)}, f32[1040]{0:T(1024)S(1)}) fusion(bf16[1040,768]{1,0:T(8,128)(2,1)} %get-tuple-element.291, bf16[1040,768]{1,0:T(8,128)(2,1)} %get-tuple-element.292, s32[1040]{0:T(1024)S(1)} %concatenate.56, s32[1040]{0:T(1024)S(1)} %concatenate.55), kind=kOutput, calls=%fused_computation.82 | convolution fusion | flops 1666743552 | bytes 3211520 | tf_op jit(solution)/shard_map/cond/branch_1_fun/dot_general | solution.py:62
  140.7 4.4 %conditional.10 = (f32[1024]{0:T(1024)S(1)}, f32[1024]{0:T(1024)S(1)}) conditional(s32[]{:T(128)} %convert_element_type.80, () %tuple.132, (s32[4]{0:T(128)S(1)}, s32[4]{0:T(128)S(1)}, bf16[1040,768]{1,0:T(8,128)(2,1)}, bf16[1040,768]{1,0:T(8,128)(2,1)}) %tuple.133), branch_computations={%region_13.14_spmd, %region_14.17_spmd} | conditional | flops 1666743552 | bytes 3269048 | solution.py:72
  140.8 4.3 %fusion.31 = (f32[1040]{0:T(1024)S(1)}, f32[1040]{0:T(1024)S(1)}) fusion(bf16[1040,768]{1,0:T(8,128)(2,1)} %get-tuple-element.287, bf16[1040,768]{1,0:T(8,128)(2,1)} %get-tuple-element.288, s32[1040]{0:T(1024)S(1)} %concatenate.54, s32[1040]{0:T(1024)S(1)} %concatenate.53), kind=kOutput, calls=%fused_computation.81 | convolution fusion | flops 1666743552 | bytes 3211520 | tf_op jit(solution)/shard_map/cond/branch_1_fun/dot_general | solution.py:62
  145.1 2.0 %collective-permute-done.8 = bf16[528,768]{1,0:T(8,128)(2,1)} collective-permute-done((bf16[528,768]{1,0:T(8,128)(2,1)S(1)}, bf16[528,768]{1,0:T(8,128)(2,1)}, u32[]{:S(2)}, u32[]{:S(2)}) %collective-permute-start.8) | collective-permute-done | bytes 811040 | tf_op jit(solution)/shard_map/ppermute | solution.py:13
  147.1 1.9 %collective-permute-start.9 = (f32[1024]{0:T(1024)S(1)}, f32[1024]{0:T(1024)S(1)}, u32[]{:S(2)}, u32[]{:S(2)}) collective-permute-start(f32[1024]{0:T(1024)S(1)} %maximum_maximum_fusion.3), channel_id=1, source_target_pairs={{0,31},{1,0},{2,1},{3,2},{4,3},{5,4},{6,5},{7,6},{8,7},{9,8},{10,9... | collective-permute-start | bytes 12296 | tf_op jit(solution)/shard_map/ppermute | solution.py:13
  149.0 1.9 %collective-permute-start.10 = (f32[1024]{0:T(1024)S(1)}, f32[1024]{0:T(1024)S(1)}, u32[]{:S(2)}, u32[]{:S(2)}) collective-permute-start(f32[1024]{0:T(1024)S(1)} %max.76), channel_id=1, source_target_pairs={{0,2},{1,3},{2,4},{3,5},{4,6},{5,7},{6,8},{7,9},{8,10},{9,11},{10,... | collective-permute-start | bytes 12296 | tf_op jit(solution)/shard_map/ppermute | solution.py:13
  150.9 1.3 convert_subtract_fusion
  152.9 3.3 %conditional.14 = (f32[1024]{0:T(1024)S(1)}, f32[512]{0:T(512)S(1)}) conditional(s32[]{:T(128)} %convert_element_type.90, () %tuple.141, (s32[2]{0:T(128)S(1)}, s32[4]{0:T(128)S(1)}, bf16[1040,768]{1,0:T(8,128)(2,1)}, bf16[528,768]{1,0:T(8,128)(2,1)}) %tuple.142), branch_computations={%region_33.34_spmd, %region_34.37_spmd} | conditional | flops 846192384 | bytes 2464176 | solution.py:72
  153.1 3.1 %fusion.35 = (f32[528]{0:T(1024)S(1)}, f32[1040]{0:T(1024)S(1)}) fusion(bf16[1040,768]{1,0:T(8,128)(2,1)} %get-tuple-element.303, bf16[528,768]{1,0:T(8,128)(2,1)} %get-tuple-element.304, s32[1040]{0:T(1024)S(1)} %concatenate.60, s32[528]{0:T(1024)S(1)} %concatenate.59), kind=kOutput, calls=%fused_computation.85 | convolution fusion | flops 846192384 | bytes 2420992 | tf_op jit(solution)/shard_map/cond/branch_1_fun/dot_general | solution.py:62
  156.2 1.8 %collective-permute-start.11 = (f32[1024]{0:T(1024)S(1)}, f32[1024]{0:T(1024)S(1)}, u32[]{:S(2)}, u32[]{:S(2)}) collective-permute-start(f32[1024]{0:T(1024)S(1)} %maximum_maximum_fusion.2), channel_id=1, source_target_pairs={{0,30},{1,31},{2,0},{3,1},{4,2},{5,3},{6,4},{7,5},{8,6},{9,7},{10,... | collective-permute-start | bytes 12296 | tf_op jit(solution)/shard_map/ppermute | solution.py:13
  158.0 1.4 fusion.21
  160.1 2.5 %conditional.15 = (f32[1024]{0:T(1024)S(1)}, f32[512]{0:T(512)S(1)}) conditional(s32[]{:T(128)} %convert_element_type.93, () %tuple.143, (s32[2]{0:T(128)S(1)}, s32[4]{0:T(128)S(1)}, bf16[1024,768]{1,0:T(8,128)(2,1)S(1)}, bf16[528,768]{1,0:T(8,128)(2,1)}) %tuple.190), branch_computations={%region_38.39_spmd, %region_39.42_spmd} | conditional | flops 833174016 | bytes 2423020 | solution.py:72
  160.3 2.3 %fusion.7 = (f32[528]{0:T(1024)S(1)}, f32[1024]{0:T(1024)S(1)}) fusion(s32[1024]{0:T(1024)S(1)} %bitcast.116, s32[528]{0:T(1024)S(1)} %concatenate.61, bf16[1024,768]{1,0:T(8,128)(2,1)S(1)} %get-tuple-element.307, bf16[528,768]{1,0:T(8,128)(2,1)} %get-tuple-element.308), kind=kOutput, calls=%fused_computation.29 | convolution fusion | flops 833174016 | bytes 2396288 | tf_op jit(solution)/shard_map/cond/branch_1_fun/dot_general | solution.py:62
  162.6 0.9 collective-permute-start.12
  163.6 2.0 %collective-permute-start.13 = (f32[512]{0:T(512)S(1)}, f32[512]{0:T(512)S(1)}, u32[]{:S(2)}, u32[]{:S(2)}) collective-permute-start(f32[512]{0:T(512)S(1)} %get-tuple-element.381), channel_id=1, source_target_pairs={{0,3},{1,4},{2,5},{3,6},{4,7},{5,8},{6,9},{7,10},{8,11},{9,12},{10... | collective-permute-start | bytes 6152 | tf_op jit(solution)/shard_map/ppermute | solution.py:13
  165.6 5.9 %collective-permute-start.14 = (f32[512]{0:T(512)S(1)}, f32[512]{0:T(512)S(1)}, u32[]{:S(2)}, u32[]{:S(2)}) collective-permute-start(f32[512]{0:T(512)S(1)} %get-tuple-element.382), channel_id=1, source_target_pairs={{0,29},{1,30},{2,31},{3,0},{4,1},{5,2},{6,3},{7,4},{8,5},{9,6},{10... | collective-permute-start | bytes 6152 | tf_op jit(solution)/shard_map/ppermute | solution.py:13
  171.5 1.4 collective-permute-done.13
  172.9 0.6 broadcast_add_fusion
  (78 shorter events, 1.0 us)
Async XLA Ops:
  0.0 1.9 %copy-start = (bf16[1024,768]{1,0:T(8,128)(2,1)S(1)}, bf16[1024,768]{1,0:T(8,128)(2,1)}, u32[]{:S(2)}) copy-start(bf16[1024,768]{1,0:T(8,128)(2,1)} %param.64) | copy-start | bytes 4718596
  1.9 0.7 copy-start.2
  2.7 62.1 %collective-permute-start = (bf16[1040,768]{1,0:T(8,128)(2,1)S(1)}, bf16[1040,768]{1,0:T(8,128)(2,1)}, u32[]{:S(2)}, u32[]{:S(2)}) collective-permute-start(bf16[1040,768]{1,0:T(8,128)(2,1)S(1)} %fusion.13), channel_id=1, source_target_pairs={{1,0},{2,1},{3,2},{4,3},{5,4},{6,5},{7,6},{8,7},{9,8},{10,9},{11,1... | collective-permute-start | bytes 4792328 | tf_op jit(solution)/shard_map/ppermute | solution.py:13
  10.4 54.3 %collective-permute-start.1 = (bf16[1040,768]{1,0:T(8,128)(2,1)S(1)}, bf16[1040,768]{1,0:T(8,128)(2,1)}, u32[]{:S(2)}, u32[]{:S(2)}) collective-permute-start(bf16[1040,768]{1,0:T(8,128)(2,1)S(1)} %fusion.13), channel_id=1, source_target_pairs={{0,1},{1,2},{2,3},{3,4},{4,5},{5,6},{6,7},{7,8},{8,9},{9,10},{10,1... | collective-permute-start | bytes 4792328 | tf_op jit(solution)/shard_map/ppermute | solution.py:13
  11.5 53.2 %collective-permute-start.2 = (bf16[512,768]{1,0:T(8,128)(2,1)S(1)}, bf16[512,768]{1,0:T(8,128)(2,1)S(1)}, u32[]{:S(2)}, u32[]{:S(2)}) collective-permute-start(bf16[512,768]{1,0:T(8,128)(2,1)S(1)} %get-tuple-element.424), channel_id=1, source_target_pairs={{0,8},{1,9},{2,10},{3,11},{4,12},{5,13},{6,14},{7,15},{8,16},{9,17... | collective-permute-start | bytes 2359304 | tf_op jit(solution)/shard_map/ppermute | solution.py:13
  64.8 54.9 %collective-permute-start.4 = (bf16[1040,768]{1,0:T(8,128)(2,1)}, bf16[1040,768]{1,0:T(8,128)(2,1)}, u32[]{:S(2)}, u32[]{:S(2)}) collective-permute-start(bf16[1040,768]{1,0:T(8,128)(2,1)} %collective-permute-done.1), channel_id=1, source_target_pairs={{0,1},{1,2},{2,3},{3,4},{4,5},{5,6},{6,7},{7,8},{8,9},{9,10},{10,1... | collective-permute-start | bytes 4792328 | tf_op jit(solution)/shard_map/ppermute | solution.py:13
  64.8 54.9 %collective-permute-start.3 = (bf16[1040,768]{1,0:T(8,128)(2,1)}, bf16[1040,768]{1,0:T(8,128)(2,1)}, u32[]{:S(2)}, u32[]{:S(2)}) collective-permute-start(bf16[1040,768]{1,0:T(8,128)(2,1)} %collective-permute-done), channel_id=1, source_target_pairs={{1,0},{2,1},{3,2},{4,3},{5,4},{6,5},{7,6},{8,7},{9,8},{10,9},{11,1... | collective-permute-start | bytes 4792328 | tf_op jit(solution)/shard_map/ppermute | solution.py:13
  70.8 48.9 %collective-permute-start.5 = (bf16[512,768]{1,0:T(8,128)(2,1)}, bf16[512,768]{1,0:T(8,128)(2,1)S(1)}, u32[]{:S(2)}, u32[]{:S(2)}) collective-permute-start(bf16[512,768]{1,0:T(8,128)(2,1)} %get-tuple-element.423), channel_id=1, source_target_pairs={{0,8},{1,9},{2,10},{3,11},{4,12},{5,13},{6,14},{7,15},{8,16},{9,17... | collective-permute-start | bytes 2359304 | tf_op jit(solution)/shard_map/ppermute | solution.py:13
  121.7 23.5 %collective-permute-start.7 = (bf16[528,768]{1,0:T(8,128)(2,1)S(1)}, bf16[528,768]{1,0:T(8,128)(2,1)}, u32[]{:S(2)}, u32[]{:S(2)}) collective-permute-start(bf16[528,768]{1,0:T(8,128)(2,1)S(1)} %pad_maximum_fusion), channel_id=1, source_target_pairs={{1,0},{2,1},{3,2},{4,3},{5,4},{6,5},{7,6},{8,7},{9,8},{10,9},{11,1... | collective-permute-start | bytes 2433032 | tf_op jit(solution)/shard_map/ppermute | solution.py:13
  124.8 22.3 %collective-permute-start.8 = (bf16[528,768]{1,0:T(8,128)(2,1)S(1)}, bf16[528,768]{1,0:T(8,128)(2,1)}, u32[]{:S(2)}, u32[]{:S(2)}) collective-permute-start(bf16[528,768]{1,0:T(8,128)(2,1)S(1)} %concatenate.68), channel_id=1, source_target_pairs={{0,1},{1,2},{2,3},{3,4},{4,5},{5,6},{6,7},{7,8},{8,9},{9,10},{10,1... | collective-permute-start | bytes 2433032 | tf_op jit(solution)/shard_map/ppermute | solution.py:13
  128.5 35.1 %collective-permute-start.6 = (f32[1024]{0:T(1024)S(1)}, f32[1024]{0:T(1024)S(1)}, u32[]{:S(2)}, u32[]{:S(2)}) collective-permute-start(f32[1024]{0:T(1024)S(1)} %max.71), channel_id=1, source_target_pairs={{0,1},{1,2},{2,3},{3,4},{4,5},{5,6},{6,7},{7,8},{8,9},{9,10},{10,1... | collective-permute-start | bytes 12296 | tf_op jit(solution)/shard_map/ppermute | solution.py:13
  147.1 18.5 %collective-permute-start.9 = (f32[1024]{0:T(1024)S(1)}, f32[1024]{0:T(1024)S(1)}, u32[]{:S(2)}, u32[]{:S(2)}) collective-permute-start(f32[1024]{0:T(1024)S(1)} %maximum_maximum_fusion.3), channel_id=1, source_target_pairs={{0,31},{1,0},{2,1},{3,2},{4,3},{5,4},{6,5},{7,6},{8,7},{9,8},{10,9... | collective-permute-start | bytes 12296 | tf_op jit(solution)/shard_map/ppermute | solution.py:13
  149.0 22.5 %collective-permute-start.10 = (f32[1024]{0:T(1024)S(1)}, f32[1024]{0:T(1024)S(1)}, u32[]{:S(2)}, u32[]{:S(2)}) collective-permute-start(f32[1024]{0:T(1024)S(1)} %max.76), channel_id=1, source_target_pairs={{0,2},{1,3},{2,4},{3,5},{4,6},{5,7},{6,8},{7,9},{8,10},{9,11},{10,... | collective-permute-start | bytes 12296 | tf_op jit(solution)/shard_map/ppermute | solution.py:13
  152.9 5.2 %copy-start.3 = (s32[1,2]{1,0:T(1,128)S(1)}, s32[1,2]{1,0:T(1,128)}, u32[]{:S(2)}) copy-start(s32[1,2]{1,0:T(1,128)} %constant.408) | copy-start | bytes 28
  152.9 7.2 %copy-start.1 = (bf16[1024,768]{1,0:T(8,128)(2,1)S(1)}, bf16[1024,768]{1,0:T(8,128)(2,1)}, u32[]{:S(2)}) copy-start(bf16[1024,768]{1,0:T(8,128)(2,1)} %constant_dynamic-update-slice_fusion) | copy-start | bytes 4718596
  156.2 15.3 %collective-permute-start.11 = (f32[1024]{0:T(1024)S(1)}, f32[1024]{0:T(1024)S(1)}, u32[]{:S(2)}, u32[]{:S(2)}) collective-permute-start(f32[1024]{0:T(1024)S(1)} %maximum_maximum_fusion.2), channel_id=1, source_target_pairs={{0,30},{1,31},{2,0},{3,1},{4,2},{5,3},{6,4},{7,5},{8,6},{9,7},{10,... | collective-permute-start | bytes 12296 | tf_op jit(solution)/shard_map/ppermute | solution.py:13
  162.6 8.9 %collective-permute-start.12 = (f32[1024]{0:T(1024)S(1)}, f32[1024]{0:T(1024)S(1)}, u32[]{:S(2)}, u32[]{:S(2)}) collective-permute-start(f32[1024]{0:T(1024)S(1)} %maximum_maximum_fusion), channel_id=1, source_target_pairs={{0,24},{1,25},{2,26},{3,27},{4,28},{5,29},{6,30},{7,31},{8,0},{9,1... | collective-permute-start | bytes 12296 | tf_op jit(solution)/shard_map/ppermute | solution.py:13
  163.6 9.4 %collective-permute-start.13 = (f32[512]{0:T(512)S(1)}, f32[512]{0:T(512)S(1)}, u32[]{:S(2)}, u32[]{:S(2)}) collective-permute-start(f32[512]{0:T(512)S(1)} %get-tuple-element.381), channel_id=1, source_target_pairs={{0,3},{1,4},{2,5},{3,6},{4,7},{5,8},{6,9},{7,10},{8,11},{9,12},{10... | collective-permute-start | bytes 6152 | tf_op jit(solution)/shard_map/ppermute | solution.py:13
  165.6 7.4 %collective-permute-start.14 = (f32[512]{0:T(512)S(1)}, f32[512]{0:T(512)S(1)}, u32[]{:S(2)}, u32[]{:S(2)}) collective-permute-start(f32[512]{0:T(512)S(1)} %get-tuple-element.382), channel_id=1, source_target_pairs={{0,29},{1,30},{2,31},{3,0},{4,1},{5,2},{6,3},{7,4},{8,5},{9,6},{10... | collective-permute-start | bytes 6152 | tf_op jit(solution)/shard_map/ppermute | solution.py:13
where the time goes:
time: 175 us; the launch traced here: 174 us
  waiting for transfers between devices  89.6 us (51%)
  starting transfers between devices  37.3 us (21%)
  matrix products  23.8 us (14%)
  other arithmetic  9.83 us (6%)
  local copies, waits for them, and re-layouts  7.1 us (4%)
  between operations  5.45 us (3%)
    ppermute x15, waiting for transfers between devices, shift(): return lax.ppermute(value, axis, pairs)  89.6 us
    ppermute x15, starting transfers between devices, shift(): return lax.ppermute(value, axis, pairs)  37.3 us
    dot_general x6, matrix products, compute(): sims = jnp.dot(a, b.T, preferred_element_type=jnp.float32)  21.8 us
    sub x4, other arithmetic, tile(): block_reach = k * blocks + jnp.array(b_blocks, jnp.int32) - lags  5.43 us
  transfers between devices with their start and end apart: 15, of which 4 were waited for; matrix products, arithmetic and copies ran while one was open for 20% of the time, Pallas kernels for 0%

commit v1 on v0

--- a/solution.py
+++ b/solution.py
@@ -109,22 +109,23 @@
 
     hops = 3
     plan = plan_of()
+    sent_ahead, sent_behind = packet, packet
     for hop in range(1, hops + 1):
         if hop < hops:
-            a_next = shift(ahead[-1], "dev", -1)
-            b_next = shift(behind[-1], "dev", 1, cyclic=True)
+            sent_ahead = shift(sent_ahead, "dev", -1)
+            sent_behind = shift(sent_behind, "dev", 1, cyclic=True)
         else:
-            a_next = shift(part(ahead[-1], low), "dev", -1)
-            b_next = shift(part(behind[-1], high), "dev", 1, cyclic=True)
+            sent_ahead = shift(part(sent_ahead, low), "dev", -1)
+            sent_behind = shift(part(sent_behind, high), "dev", 1, cyclic=True)
         ready = [entry for entry in plan if entry[0] == hop - 1]
         pieces = [tile(fetch(e[1]), e[2], fetch(e[3]), e[4], e[5], e[6]) for e in ready]
         if hop == 1:
-            a_next, b_next, first, best = lax.optimization_barrier((a_next, b_next, far_halves[0], best))
+            a_next, b_next, first, best = lax.optimization_barrier((sent_ahead, sent_behind, far_halves[0], best))
         elif hop == 2:
-            a_next, b_next, second, pieces = lax.optimization_barrier((a_next, b_next, far_halves[1], pieces))
+            a_next, b_next, second, pieces = lax.optimization_barrier((sent_ahead, sent_behind, far_halves[1], pieces))
             far = jnp.concatenate([first, second], axis=0)
         else:
-            a_next, b_next, pieces = lax.optimization_barrier((a_next, b_next, pieces))
+            a_next, b_next, pieces = lax.optimization_barrier((sent_ahead, sent_behind, pieces))
         for e, (row_part, column_part) in zip(ready, pieces):
             gather(e[7], e[2], row_part)
             gather(e[8], e[4], column_part)

time: 175 us -> 187 us (1.069)
  matrix products: 23.8 us -> 5.53 us
  starting transfers between devices: 37.3 us -> 53.6 us
  waiting for transfers between devices: 89.6 us -> 103 us
    dot_general x6 -> x1, matrix products: 21.8 us -> 3.48 us  [compute(): sims = jnp.dot(a, b.T, preferred_element_type=jnp.float32)]
    ppermute x15, starting transfers between devices: 37.3 us -> 53.6 us  [shift(): return lax.ppermute(value, axis, pairs)]
    ppermute x15, waiting for transfers between devices: 89.6 us -> 103 us  [shift(): return lax.ppermute(value, axis, pairs)]
  transfers between devices with their start and end apart: 15 -> 15, of which waited for: 4 -> 4; matrix products, arithmetic and copies ran while one was open for 20% -> 11% of each run, Pallas kernels for 0% -> 0%
where the time goes in v1:
time: 187 us; the launch traced here: 185 us
  waiting for transfers between devices  103 us (55%)
  starting transfers between devices  53.6 us (29%)
  other arithmetic  9.79 us (5%)
  local copies, waits for them, and re-layouts  7.37 us (4%)
  matrix products  5.53 us (3%)
  between operations  5.45 us (3%)
    ppermute x15, waiting for transfers between devices, shift(): return lax.ppermute(value, axis, pairs)  103 us
    ppermute x15, starting transfers between devices, shift(): return lax.ppermute(value, axis, pairs)  53.6 us
    sub x4, other arithmetic, tile(): block_reach = k * blocks + jnp.array(b_blocks, jnp.int32) - lags  5.39 us
  transfers between devices with their start and end apart: 15, of which 4 were waited for; matrix products, arithmetic and copies ran while one was open for 11% of the time, Pallas kernels for 0%

profile of v1, /device:TPU:4, one launch (start us, length us, event | category | flops | bytes accessed | tf_op | source)
XLA Modules:
  0.0 185.1 jit_solution(18316514983093397975)
XLA Ops:
  0.0 1.9 %fusion.11 = f32[1024]{0:T(1024)S(1)} fusion(bf16[1024,768]{1,0:T(8,128)(2,1)} %param.64), kind=kLoop, calls=%fused_computation.40 | loop fusion | flops 2358272 | bytes 1576960 | tf_op jit(solution)/shard_map/reduce_sum | solution.py:18
  1.9 0.0 copy-start.2
  1.9 0.3 fusion.12
  2.3 0.3 copy-done.2
  2.6 0.1 fusion.13
  2.7 7.7 %collective-permute-start = (bf16[1040,768]{1,0:T(8,128)(2,1)S(1)}, bf16[1040,768]{1,0:T(8,128)(2,1)}, u32[]{:S(2)}, u32[]{:S(2)}) collective-permute-start(bf16[1040,768]{1,0:T(8,128)(2,1)S(1)} %fusion.13), channel_id=1, source_target_pairs={{1,0},{2,1},{3,2},{4,3},{5,4},{6,5},{7,6},{8,7},{9,8},{10,9},{11,1... | collective-permute-start | bytes 4792328 | tf_op jit(solution)/shard_map/ppermute | solution.py:13
  10.4 0.1 collective-permute-start.1
  10.5 34.1 %collective-permute-done = bf16[1040,768]{1,0:T(8,128)(2,1)} collective-permute-done((bf16[1040,768]{1,0:T(8,128)(2,1)S(1)}, bf16[1040,768]{1,0:T(8,128)(2,1)}, u32[]{:S(2)}, u32[]{:S(2)}) %collective-permute-start) | collective-permute-done | bytes 1597472 | tf_op jit(solution)/shard_map/ppermute | solution.py:13
  44.6 6.6 %collective-permute-start.3 = (bf16[1040,768]{1,0:T(8,128)(2,1)}, bf16[1040,768]{1,0:T(8,128)(2,1)}, u32[]{:S(2)}, u32[]{:S(2)}) collective-permute-start(bf16[1040,768]{1,0:T(8,128)(2,1)} %collective-permute-done), channel_id=1, source_target_pairs={{1,0},{2,1},{3,2},{4,3},{5,4},{6,5},{7,6},{8,7},{9,8},{10,9},{11,1... | collective-permute-start | bytes 4792328 | tf_op jit(solution)/shard_map/ppermute | solution.py:13
  51.2 0.1 collective-permute-start.4
  51.3 1.1 fusion.36
  52.4 1.5 collective-permute-start.2
  53.9 0.0 collective-permute-start.5
  53.9 0.1 broadcast_bitcast_fusion.16
  54.0 2.1 %select_reduce_fusion = f32[1024]{0:T(1024)S(1)} fusion(s32[1024]{0:T(1024)S(1)} %bitcast.116, bf16[1024,768]{1,0:T(8,128)(2,1)S(1)} %fusion.12), kind=kOutput, calls=%fused_computation.33 | convolution fusion | flops 1616903168 | bytes 1581056 | tf_op jit(solution)/shard_map/dot_general | solution.py:35
  56.0 50.0 %collective-permute-done.2 = bf16[512,768]{1,0:T(8,128)(2,1)S(1)} collective-permute-done((bf16[512,768]{1,0:T(8,128)(2,1)S(1)}, bf16[512,768]{1,0:T(8,128)(2,1)S(1)}, u32[]{:S(2)}, u32[]{:S(2)}) %collective-permute-start.2) | collective-permute-done | bytes 786464 | tf_op jit(solution)/shard_map/ppermute | solution.py:13
  106.1 0.0 collective-permute-done.3
  106.1 1.5 slice.193
  107.6 0.7 slice.194
  108.3 0.1 pad_maximum_fusion
  108.4 1.9 %collective-permute-start.7 = (bf16[528,768]{1,0:T(8,128)(2,1)S(1)}, bf16[528,768]{1,0:T(8,128)(2,1)}, u32[]{:S(2)}, u32[]{:S(2)}) collective-permute-start(bf16[528,768]{1,0:T(8,128)(2,1)S(1)} %pad_maximum_fusion), channel_id=1, source_target_pairs={{1,0},{2,1},{3,2},{4,3},{5,4},{6,5},{7,6},{8,7},{9,8},{10,9},{11,1... | collective-permute-start | bytes 2433032 | tf_op jit(solution)/shard_map/ppermute | solution.py:13
  110.3 1.2 concatenate.70
  111.5 2.1 %collective-permute-start.8 = (bf16[528,768]{1,0:T(8,128)(2,1)S(1)}, bf16[528,768]{1,0:T(8,128)(2,1)}, u32[]{:S(2)}, u32[]{:S(2)}) collective-permute-start(bf16[528,768]{1,0:T(8,128)(2,1)S(1)} %concatenate.70), channel_id=1, source_target_pairs={{0,1},{1,2},{2,3},{3,4},{4,5},{5,6},{6,7},{7,8},{8,9},{9,10},{10,1... | collective-permute-start | bytes 2433032 | tf_op jit(solution)/shard_map/ppermute | solution.py:13
  113.6 1.4 fusion.18
  116.9 3.6 %conditional.8 = (f32[1024]{0:T(1024)S(1)}, f32[1024]{0:T(1024)S(1)}) conditional(s32[]{:T(128)} %convert_element_type.76, () %tuple.127, (s32[4]{0:T(128)S(1)}, s32[4]{0:T(128)S(1)}, bf16[1024,768]{1,0:T(8,128)(2,1)S(1)}, bf16[1040,768]{1,0:T(8,128)(2,1)}) %tuple.128), branch_computations={%region_3.4_spmd, %region_4.7_spmd} | conditional | flops 1641101312 | bytes 3227892 | solution.py:72
  116.9 0.1 broadcast_bitcast_fusion
  117.0 3.5 %fusion.29 = (f32[1040]{0:T(1024)S(1)}, f32[1024]{0:T(1024)S(1)}) fusion(bf16[1024,768]{1,0:T(8,128)(2,1)S(1)} %get-tuple-element.279, bf16[1040,768]{1,0:T(8,128)(2,1)} %get-tuple-element.280, s32[1024]{0:T(1024)S(1)} %bitcast.118, s32[1040]{0:T(1024)S(1)} %concatenate.50), kind=kOutput, calls=%fused_computation.79 | convolution fusion | flops 1641101312 | bytes 3186816 | tf_op jit(solution)/shard_map/cond/branch_1_fun/dot_general | solution.py:62
  120.5 1.2 constant_dynamic-update-slice_fusion.1
  121.6 17.4 %collective-permute-done.5 = bf16[512,768]{1,0:T(8,128)(2,1)} collective-permute-done((bf16[512,768]{1,0:T(8,128)(2,1)}, bf16[512,768]{1,0:T(8,128)(2,1)}, u32[]{:S(2)}, u32[]{:S(2)}) %collective-permute-start.5) | collective-permute-done | bytes 786464 | tf_op jit(solution)/shard_map/ppermute | solution.py:13
  139.1 1.9 %collective-permute-start.6 = (f32[1024]{0:T(1024)S(1)}, f32[1024]{0:T(1024)S(1)}, u32[]{:S(2)}, u32[]{:S(2)}) collective-permute-start(f32[1024]{0:T(1024)S(1)} %max.71), channel_id=1, source_target_pairs={{0,1},{1,2},{2,3},{3,4},{4,5},{5,6},{6,7},{7,8},{8,9},{9,10},{10,1... | collective-permute-start | bytes 12296 | tf_op jit(solution)/shard_map/ppermute | solution.py:13
  141.0 1.3 fusion.19
  143.0 1.2 constant_dynamic-update-slice_fusion
  144.2 1.4 fusion.25
  146.9 0.2 conditional.13
  147.2 0.0 collective-permute-done.7
  147.3 4.2 %collective-permute-start.9 = (f32[1024]{0:T(1024)S(1)}, f32[1024]{0:T(1024)S(1)}, u32[]{:S(2)}, u32[]{:S(2)}) collective-permute-start(f32[1024]{0:T(1024)S(1)} %maximum_maximum_fusion.3), channel_id=1, source_target_pairs={{0,31},{1,0},{2,1},{3,2},{4,3},{5,4},{6,5},{7,6},{8,7},{9,8},{10,9... | collective-permute-start | bytes 12296 | tf_op jit(solution)/shard_map/ppermute | solution.py:13
  151.5 1.9 %collective-permute-start.10 = (f32[1024]{0:T(1024)S(1)}, f32[1024]{0:T(1024)S(1)}, u32[]{:S(2)}, u32[]{:S(2)}) collective-permute-start(f32[1024]{0:T(1024)S(1)} %max.76), channel_id=1, source_target_pairs={{0,2},{1,3},{2,4},{3,5},{4,6},{5,7},{6,8},{7,9},{8,10},{9,11},{10,... | collective-permute-start | bytes 12296 | tf_op jit(solution)/shard_map/ppermute | solution.py:13
  153.4 1.3 convert_subtract_fusion
  155.3 0.0 copy-start.3
  155.4 5.1 %collective-permute-start.11 = (f32[1024]{0:T(1024)S(1)}, f32[1024]{0:T(1024)S(1)}, u32[]{:S(2)}, u32[]{:S(2)}) collective-permute-start(f32[1024]{0:T(1024)S(1)} %maximum_maximum_fusion.2), channel_id=1, source_target_pairs={{0,30},{1,31},{2,0},{3,1},{4,2},{5,3},{6,4},{7,5},{8,6},{9,7},{10,... | collective-permute-start | bytes 12296 | tf_op jit(solution)/shard_map/ppermute | solution.py:13
  160.5 1.4 fusion.21
  162.6 12.5 %collective-permute-start.12 = (f32[1024]{0:T(1024)S(1)}, f32[1024]{0:T(1024)S(1)}, u32[]{:S(2)}, u32[]{:S(2)}) collective-permute-start(f32[1024]{0:T(1024)S(1)} %maximum_maximum_fusion), channel_id=1, source_target_pairs={{0,24},{1,25},{2,26},{3,27},{4,28},{5,29},{6,30},{7,31},{8,0},{9,1... | collective-permute-start | bytes 12296 | tf_op jit(solution)/shard_map/ppermute | solution.py:13
  175.1 0.0 collective-permute-done.6
  175.2 1.9 %collective-permute-start.13 = (f32[512]{0:T(512)S(1)}, f32[512]{0:T(512)S(1)}, u32[]{:S(2)}, u32[]{:S(2)}) collective-permute-start(f32[512]{0:T(512)S(1)} %get-tuple-element.381), channel_id=1, source_target_pairs={{0,3},{1,4},{2,5},{3,6},{4,7},{5,8},{6,9},{7,10},{8,11},{9,12},{10... | collective-permute-start | bytes 6152 | tf_op jit(solution)/shard_map/ppermute | solution.py:13
  177.1 6.0 %collective-permute-start.14 = (f32[512]{0:T(512)S(1)}, f32[512]{0:T(512)S(1)}, u32[]{:S(2)}, u32[]{:S(2)}) collective-permute-start(f32[512]{0:T(512)S(1)} %get-tuple-element.382), channel_id=1, source_target_pairs={{0,29},{1,30},{2,31},{3,0},{4,1},{5,2},{6,3},{7,4},{8,5},{9,6},{10... | collective-permute-start | bytes 6152 | tf_op jit(solution)/shard_map/ppermute | solution.py:13
  183.1 0.0 collective-permute-done.10
  183.1 1.4 collective-permute-done.13
  184.5 0.6 broadcast_add_fusion
  (48 shorter events, 0.4 us)
Async XLA Ops:
  0.0 1.9 %copy-start = (bf16[1024,768]{1,0:T(8,128)(2,1)S(1)}, bf16[1024,768]{1,0:T(8,128)(2,1)}, u32[]{:S(2)}) copy-start(bf16[1024,768]{1,0:T(8,128)(2,1)} %param.64) | copy-start | bytes 4718596
  1.9 0.7 copy-start.2
  2.7 41.9 %collective-permute-start = (bf16[1040,768]{1,0:T(8,128)(2,1)S(1)}, bf16[1040,768]{1,0:T(8,128)(2,1)}, u32[]{:S(2)}, u32[]{:S(2)}) collective-permute-start(bf16[1040,768]{1,0:T(8,128)(2,1)S(1)} %fusion.13), channel_id=1, source_target_pairs={{1,0},{2,1},{3,2},{4,3},{5,4},{6,5},{7,6},{8,7},{9,8},{10,9},{11,1... | collective-permute-start | bytes 4792328 | tf_op jit(solution)/shard_map/ppermute | solution.py:13
  10.4 40.8 %collective-permute-start.1 = (bf16[1040,768]{1,0:T(8,128)(2,1)S(1)}, bf16[1040,768]{1,0:T(8,128)(2,1)}, u32[]{:S(2)}, u32[]{:S(2)}) collective-permute-start(bf16[1040,768]{1,0:T(8,128)(2,1)S(1)} %fusion.13), channel_id=1, source_target_pairs={{0,1},{1,2},{2,3},{3,4},{4,5},{5,6},{6,7},{7,8},{8,9},{9,10},{10,1... | collective-permute-start | bytes 4792328 | tf_op jit(solution)/shard_map/ppermute | solution.py:13
  44.6 61.5 %collective-permute-start.3 = (bf16[1040,768]{1,0:T(8,128)(2,1)}, bf16[1040,768]{1,0:T(8,128)(2,1)}, u32[]{:S(2)}, u32[]{:S(2)}) collective-permute-start(bf16[1040,768]{1,0:T(8,128)(2,1)} %collective-permute-done), channel_id=1, source_target_pairs={{1,0},{2,1},{3,2},{4,3},{5,4},{6,5},{7,6},{8,7},{9,8},{10,9},{11,1... | collective-permute-start | bytes 4792328 | tf_op jit(solution)/shard_map/ppermute | solution.py:13
  51.2 59.1 %collective-permute-start.4 = (bf16[1040,768]{1,0:T(8,128)(2,1)}, bf16[1040,768]{1,0:T(8,128)(2,1)}, u32[]{:S(2)}, u32[]{:S(2)}) collective-permute-start(bf16[1040,768]{1,0:T(8,128)(2,1)} %collective-permute-done.1), channel_id=1, source_target_pairs={{0,1},{1,2},{2,3},{3,4},{4,5},{5,6},{6,7},{7,8},{8,9},{9,10},{10,1... | collective-permute-start | bytes 4792328 | tf_op jit(solution)/shard_map/ppermute | solution.py:13
  52.4 53.7 %collective-permute-start.2 = (bf16[512,768]{1,0:T(8,128)(2,1)S(1)}, bf16[512,768]{1,0:T(8,128)(2,1)S(1)}, u32[]{:S(2)}, u32[]{:S(2)}) collective-permute-start(bf16[512,768]{1,0:T(8,128)(2,1)S(1)} %get-tuple-element.423), channel_id=1, source_target_pairs={{0,8},{1,9},{2,10},{3,11},{4,12},{5,13},{6,14},{7,15},{8,16},{9,17... | collective-permute-start | bytes 2359304 | tf_op jit(solution)/shard_map/ppermute | solution.py:13
  53.9 85.2 %collective-permute-start.5 = (bf16[512,768]{1,0:T(8,128)(2,1)}, bf16[512,768]{1,0:T(8,128)(2,1)}, u32[]{:S(2)}, u32[]{:S(2)}) collective-permute-start(bf16[512,768]{1,0:T(8,128)(2,1)} %get-tuple-element.424), channel_id=1, source_target_pairs={{0,8},{1,9},{2,10},{3,11},{4,12},{5,13},{6,14},{7,15},{8,16},{9,17... | collective-permute-start | bytes 2359304 | tf_op jit(solution)/shard_map/ppermute | solution.py:13
  106.1 1.5 copy-start.1
  108.4 38.9 %collective-permute-start.7 = (bf16[528,768]{1,0:T(8,128)(2,1)S(1)}, bf16[528,768]{1,0:T(8,128)(2,1)}, u32[]{:S(2)}, u32[]{:S(2)}) collective-permute-start(bf16[528,768]{1,0:T(8,128)(2,1)S(1)} %pad_maximum_fusion), channel_id=1, source_target_pairs={{1,0},{2,1},{3,2},{4,3},{5,4},{6,5},{7,6},{8,7},{9,8},{10,9},{11,1... | collective-permute-start | bytes 2433032 | tf_op jit(solution)/shard_map/ppermute | solution.py:13
  111.5 35.7 %collective-permute-start.8 = (bf16[528,768]{1,0:T(8,128)(2,1)S(1)}, bf16[528,768]{1,0:T(8,128)(2,1)}, u32[]{:S(2)}, u32[]{:S(2)}) collective-permute-start(bf16[528,768]{1,0:T(8,128)(2,1)S(1)} %concatenate.70), channel_id=1, source_target_pairs={{0,1},{1,2},{2,3},{3,4},{4,5},{5,6},{6,7},{7,8},{8,9},{9,10},{10,1... | collective-permute-start | bytes 2433032 | tf_op jit(solution)/shard_map/ppermute | solution.py:13
  139.1 36.1 %collective-permute-start.6 = (f32[1024]{0:T(1024)S(1)}, f32[1024]{0:T(1024)S(1)}, u32[]{:S(2)}, u32[]{:S(2)}) collective-permute-start(f32[1024]{0:T(1024)S(1)} %max.71), channel_id=1, source_target_pairs={{0,1},{1,2},{2,3},{3,4},{4,5},{5,6},{6,7},{7,8},{8,9},{9,10},{10,1... | collective-permute-start | bytes 12296 | tf_op jit(solution)/shard_map/ppermute | solution.py:13
  147.3 29.8 %collective-permute-start.9 = (f32[1024]{0:T(1024)S(1)}, f32[1024]{0:T(1024)S(1)}, u32[]{:S(2)}, u32[]{:S(2)}) collective-permute-start(f32[1024]{0:T(1024)S(1)} %maximum_maximum_fusion.3), channel_id=1, source_target_pairs={{0,31},{1,0},{2,1},{3,2},{4,3},{5,4},{6,5},{7,6},{8,7},{9,8},{10,9... | collective-permute-start | bytes 12296 | tf_op jit(solution)/shard_map/ppermute | solution.py:13
  151.5 31.6 %collective-permute-start.10 = (f32[1024]{0:T(1024)S(1)}, f32[1024]{0:T(1024)S(1)}, u32[]{:S(2)}, u32[]{:S(2)}) collective-permute-start(f32[1024]{0:T(1024)S(1)} %max.76), channel_id=1, source_target_pairs={{0,2},{1,3},{2,4},{3,5},{4,6},{5,7},{6,8},{7,9},{8,10},{9,11},{10,... | collective-permute-start | bytes 12296 | tf_op jit(solution)/shard_map/ppermute | solution.py:13
  155.3 5.2 %copy-start.3 = (s32[1,2]{1,0:T(1,128)S(1)}, s32[1,2]{1,0:T(1,128)}, u32[]{:S(2)}) copy-start(s32[1,2]{1,0:T(1,128)} %constant.408) | copy-start | bytes 28
  155.4 27.7 %collective-permute-start.11 = (f32[1024]{0:T(1024)S(1)}, f32[1024]{0:T(1024)S(1)}, u32[]{:S(2)}, u32[]{:S(2)}) collective-permute-start(f32[1024]{0:T(1024)S(1)} %maximum_maximum_fusion.2), channel_id=1, source_target_pairs={{0,30},{1,31},{2,0},{3,1},{4,2},{5,3},{6,4},{7,5},{8,6},{9,7},{10,... | collective-permute-start | bytes 12296 | tf_op jit(solution)/shard_map/ppermute | solution.py:13
  162.6 20.5 %collective-permute-start.12 = (f32[1024]{0:T(1024)S(1)}, f32[1024]{0:T(1024)S(1)}, u32[]{:S(2)}, u32[]{:S(2)}) collective-permute-start(f32[1024]{0:T(1024)S(1)} %maximum_maximum_fusion), channel_id=1, source_target_pairs={{0,24},{1,25},{2,26},{3,27},{4,28},{5,29},{6,30},{7,31},{8,0},{9,1... | collective-permute-start | bytes 12296 | tf_op jit(solution)/shard_map/ppermute | solution.py:13
  175.2 9.4 %collective-permute-start.13 = (f32[512]{0:T(512)S(1)}, f32[512]{0:T(512)S(1)}, u32[]{:S(2)}, u32[]{:S(2)}) collective-permute-start(f32[512]{0:T(512)S(1)} %get-tuple-element.381), channel_id=1, source_target_pairs={{0,3},{1,4},{2,5},{3,6},{4,7},{5,8},{6,9},{7,10},{8,11},{9,12},{10... | collective-permute-start | bytes 6152 | tf_op jit(solution)/shard_map/ppermute | solution.py:13
  177.1 7.5 %collective-permute-start.14 = (f32[512]{0:T(512)S(1)}, f32[512]{0:T(512)S(1)}, u32[]{:S(2)}, u32[]{:S(2)}) collective-permute-start(f32[512]{0:T(512)S(1)} %get-tuple-element.382), channel_id=1, source_target_pairs={{0,29},{1,30},{2,31},{3,0},{4,1},{5,2},{6,3},{7,4},{8,5},{9,6},{10... | collective-permute-start | bytes 6152 | tf_op jit(solution)/shard_map/ppermute | solution.py:13
